TPU v7x, 256 devices: a whole 4x4x8 slice. The times are simulated.
256 devices in a mesh: dp: 4 (over z_lo, core), cp: 16 (over y, z_hi), tp: 4 (over x).
Axes of the slice: x: 4, y: 4, z: 8 (z_hi: 4, z_lo: 2; z = z_hi * 2 + z_lo), core: 2. Of those that a mesh axis runs over, the one named last changes fastest.
Arguments:
- hidden: bfloat16 [4, 2048, 8192], P('dp', 'cp'), may hold values from -6 to 6
- query: bfloat16 [4, 2048, 8192], P('dp', 'cp', 'tp'), may hold values from -360 to 360
- grad_out: bfloat16 [4, 2048, 8192], P('dp', 'cp', 'tp'), may hold values from -6 to 6
- k_weight: bfloat16 [8192, 1024], P('dp', 'tp'), may hold values from -0.0625 to 0.0625
- v_weight: bfloat16 [8192, 1024], P('dp', 'tp'), may hold values from -0.0625 to 0.0625
- doc_starts: int32 [4, 4], P('dp'), may hold values from 0 to 2047, as said below
Outputs:
- attn_out: bfloat16 [4, 2048, 8192], P('dp', 'cp', 'tp')
- query_grad: bfloat16 [4, 2048, 8192], P('dp', 'cp', 'tp')
- k_weight_grad: float32 [8192, 1024], P(('dp', 'cp'), 'tp')
- v_weight_grad: float32 [8192, 1024], P(('dp', 'cp'), 'tp')
Inputs may be any that keep to these rules, and one draw needn't show every extreme that they name: `doc_starts`: in each sequence the starts strictly increase and the first is 0.
All inputs are finite; a program needn't handle non-finite values.
Results may differ from a plain program's by a relative error of at most 0.04.
The roundings to bfloat16 on the way count: a program that leaves them out, or rounds other values in their place, can miss the bound.
Values may be sent and summed in bfloat16 or wider, within the bound.
No kernel may reach another device: no remote copies, remote signals or barrier semaphores. Data moves between devices by JAX's collectives and lax.ppermute only.
A program may use at most 128 MiB of HBM per device.

v0:
```python
import math
import jax
import jax.numpy as jnp
from jax import lax
from jax.sharding import PartitionSpec as P

DH = 128
NEG_BIG = -1e30


def place(rows, tok_rows, seq_rows):
    stretch = rows // tok_rows
    within = rows % tok_rows
    half_rows = tok_rows // 2
    return jnp.where(
        within < half_rows,
        stretch * half_rows + within,
        seq_rows - (stretch + 1) * half_rows + within - half_rows,
    )


def doc_index(positions, starts):
    return jnp.sum((starts[None, :] <= positions[:, None]).astype(jnp.int32), axis=1) - 1


def sweep(update, initial, all_keys, all_vals, span):

    def step_fn(block_index, running):
        first_row = block_index * span
        pieces = (
            lax.dynamic_slice_in_dim(all_keys, first_row, span, 0),
            lax.dynamic_slice_in_dim(all_vals, first_row, span, 0),
        )
        return update(running, pieces, first_row)

    return lax.fori_loop(0, all_keys.shape[0] // span, step_fn, initial)


def on_device(hidden, query, grad_out, k_weight, v_weight, doc_starts):
    inputs = hidden[0]
    tok_rows = inputs.shape[0]
    cp_count = lax.axis_size("cp")
    seq_rows = tok_rows * cp_count
    score_scale = DH ** (-0.5)
    kv_width = k_weight.shape[1]
    kv_heads = kv_width // DH
    per_group = query.shape[2] // DH // kv_heads
    starts = doc_starts[0]
    own_rows = lax.axis_index("cp") * tok_rows + jnp.arange(tok_rows, dtype=jnp.int32)
    own_place = place(own_rows, tok_rows, seq_rows)
    own_doc = doc_index(own_place, starts)

    def allowed_pairs(first_row, piece_rows):
        key_place = place(first_row + jnp.arange(piece_rows, dtype=jnp.int32), tok_rows, seq_rows)
        key_doc = doc_index(key_place, starts)
        return (key_place[None, :] <= own_place[:, None]) & (key_doc[None, :] == own_doc[:, None])

    pieces = (
        lax.all_gather(k_weight, "dp", axis=0, tiled=True),
        lax.all_gather(v_weight, "dp", axis=0, tiled=True),
    )
    columns = inputs
    key_sums = jnp.dot(columns, pieces[0], preferred_element_type=jnp.float32)
    value_sums = jnp.dot(columns, pieces[1], preferred_element_type=jnp.float32)
    keys = key_sums.astype(jnp.bfloat16)
    values = value_sums.astype(jnp.bfloat16)
    queries = query[0].reshape(tok_rows, kv_heads, per_group, DH)
    upstream = grad_out[0].reshape(tok_rows, kv_heads, per_group, DH)

    def totals_step(running, pieces, first_row):
        key_piece = pieces[0]
        piece_rows = key_piece.shape[0]
        allowed = allowed_pairs(first_row, piece_rows)
        top_score, denom = running
        key_heads = key_piece.reshape(piece_rows, kv_heads, DH)
        scores = (
            jnp.einsum("qgid,kgd->giqk", queries, key_heads, preferred_element_type=jnp.float32)
            * score_scale
        )
        scores = jnp.where(allowed, scores, NEG_BIG)
        fresh_top = jnp.maximum(top_score, jnp.max(scores, axis=-1))
        expos = jnp.where(allowed, jnp.exp(scores - fresh_top[..., None]), 0.0)
        denom = denom * jnp.exp(top_score - fresh_top) + jnp.sum(expos, axis=-1)
        return (fresh_top, denom)

    start_totals = (
        jnp.full((kv_heads, per_group, tok_rows), NEG_BIG, jnp.float32),
        jnp.zeros((kv_heads, per_group, tok_rows), jnp.float32),
    )
    span = tok_rows * math.gcd(cp_count, max(1, 512 // tok_rows))
    all_keys, all_vals = (
        lax.all_gather(keys, "cp", axis=0, tiled=True),
        lax.all_gather(values, "cp", axis=0, tiled=True),
    )
    top_score, denom = sweep(totals_step, start_totals, all_keys, all_vals, span)
    log_total = top_score + jnp.log(denom)

    def output_step(running, pieces, first_row):
        key_piece, value_piece = pieces
        piece_rows = key_piece.shape[0]
        allowed = allowed_pairs(first_row, piece_rows)
        key_heads = key_piece.reshape(piece_rows, kv_heads, DH)
        value_heads = value_piece.reshape(piece_rows, kv_heads, DH)
        scores = (
            jnp.einsum("qgid,kgd->giqk", queries, key_heads, preferred_element_type=jnp.float32)
            * score_scale
        )
        weights_bf = jnp.where(allowed, jnp.exp(scores - log_total[..., None]), 0.0).astype(
            jnp.bfloat16
        )
        return running + jnp.einsum(
            "giqk,kgd->qgid", weights_bf, value_heads, preferred_element_type=jnp.float32
        )

    start_output = jnp.zeros((tok_rows, kv_heads, per_group, DH), jnp.float32)
    accum = sweep(output_step, start_output, all_keys, all_vals, span)
    out_rows = accum.astype(jnp.bfloat16)
    delta = jnp.transpose(
        jnp.sum(upstream.astype(jnp.float32) * out_rows.astype(jnp.float32), axis=-1), (1, 2, 0)
    )

    def backward(running, pieces, first_row):
        key_piece, value_piece = pieces
        piece_rows = key_piece.shape[0]
        allowed = allowed_pairs(first_row, piece_rows)
        query_acc, key_term, value_term = running
        key_heads = key_piece.reshape(piece_rows, kv_heads, DH)
        value_heads = value_piece.reshape(piece_rows, kv_heads, DH)
        scores = (
            jnp.einsum("qgid,kgd->giqk", queries, key_heads, preferred_element_type=jnp.float32)
            * score_scale
        )
        weights = jnp.where(allowed, jnp.exp(scores - log_total[..., None]), 0.0)
        weights_bf = weights.astype(jnp.bfloat16)
        prob_grads = jnp.einsum(
            "qgid,kgd->giqk", upstream, value_heads, preferred_element_type=jnp.float32
        )
        score_grads = (weights * (prob_grads - delta[..., None])).astype(jnp.bfloat16)
        query_acc = (
            query_acc
            + jnp.einsum(
                "giqk,kgd->qgid", score_grads, key_heads, preferred_element_type=jnp.float32
            )
            * score_scale
        )
        key_piece_grad = (
            jnp.einsum("giqk,qgid->kgd", score_grads, queries, preferred_element_type=jnp.float32)
            * score_scale
        )
        value_piece_grad = jnp.einsum(
            "giqk,qgid->kgd", weights_bf, upstream, preferred_element_type=jnp.float32
        )
        key_term = lax.dynamic_update_slice_in_dim(
            key_term, key_piece_grad.reshape(piece_rows, kv_width), first_row, 0
        )
        value_term = lax.dynamic_update_slice_in_dim(
            value_term, value_piece_grad.reshape(piece_rows, kv_width), first_row, 0
        )
        return (query_acc, key_term, value_term)

    start_backward = (
        jnp.zeros((tok_rows, kv_heads, per_group, DH), jnp.float32),
        jnp.zeros((seq_rows, kv_width), jnp.float32),
        jnp.zeros((seq_rows, kv_width), jnp.float32),
    )
    query_acc, key_term, value_term = sweep(backward, start_backward, all_keys, all_vals, span)
    key_sum, value_sum = (
        lax.psum_scatter(
            key_term.astype(jnp.bfloat16), "cp", scatter_dimension=0, tiled=True
        ).astype(jnp.float32),
        lax.psum_scatter(
            value_term.astype(jnp.bfloat16), "cp", scatter_dimension=0, tiled=True
        ).astype(jnp.float32),
    )
    both_grads = jnp.concatenate(
        [key_sum.astype(jnp.bfloat16), value_sum.astype(jnp.bfloat16)], axis=1
    )
    columns = inputs
    result = lax.psum_scatter(
        jnp.dot(columns.T, both_grads, preferred_element_type=jnp.float32),
        ("dp", "cp"),
        scatter_dimension=0,
        tiled=True,
    )
    attn_rows = out_rows.reshape(1, tok_rows, kv_heads * per_group * DH)
    query_rows = query_acc.astype(jnp.bfloat16).reshape(1, tok_rows, kv_heads * per_group * DH)
    return (attn_rows, query_rows, result[:, :kv_width], result[:, kv_width:])


def solution(mesh):
    placed = (
        P("dp", "cp", None),
        P("dp", "cp", "tp"),
        P("dp", "cp", "tp"),
        P("dp", "tp"),
        P("dp", "tp"),
        P("dp", None),
    )
    return jax.shard_map(
        on_device,
        mesh=mesh,
        in_specs=placed,
        out_specs=(
            P("dp", "cp", "tp"),
            P("dp", "cp", "tp"),
            P(("dp", "cp"), "tp"),
            P(("dp", "cp"), "tp"),
        ),
        check_vma=False,
    )
```

profile of v0, /device:TPU:36, one launch (start us, length us, event | category | flops | bytes accessed | tf_op | source)
XLA Modules:
  0.0 896.1 jit_solution(16444612808211321503)
XLA Ops:
  8.7 51.0 %all-gather.9.cloned.1.call-done = bf16[8192,256]{1,0:T(8,128)(2,1)} async-done(((bf16[2048,256]{1,0:T(8,128)(2,1)}), bf16[8192,256]{1,0:T(8,128)(2,1)}) %all-gather.9.cloned.1.call-update) | async-done | bytes 4194320 | tf_op jit(solution)/shard_map/all_gather | solution.py:59
  59.8 3.5 fusion.43
  64.0 2.0 copy.106
  66.2 44.9 %all-gather.5.cloned.1.call-done = bf16[8192,256]{1,0:T(8,128)(2,1)} async-done(((bf16[2048,256]{1,0:T(8,128)(2,1)}), bf16[8192,256]{1,0:T(8,128)(2,1)}) %all-gather.5.cloned.1.call-update) | async-done | bytes 4194320 | tf_op jit(solution)/shard_map/all_gather | solution.py:60
  111.0 3.5 fusion.40
  114.6 53.1 %all-gather.11.cloned.1.call-done = bf16[2048,256]{1,0:T(8,128)(2,1)} async-done(((bf16[128,256]{1,0:T(8,128)(2,1)}), bf16[2048,256]{1,0:T(8,128)(2,1)}) %all-gather.11.cloned.1.call-update) | async-done | bytes 1048592 | tf_op jit(solution)/shard_map/all_gather | solution.py:92
  167.7 2.3 copy.103
  170.0 12.9 %while.57 = (s32[]{:T(128)}, f32[2,8,128]{2,1,0:T(8,128)S(1)}, f32[2,8,128]{2,1,0:T(8,128)S(1)}, s32[1,4]{1,0:T(1,128)S(1)}, s32[128]{0:T(128)S(1)}, /*index=5*/...) while((s32[]{:T(128)}, f32[2,8,128]{2,1,0:T(8,128)S(1)}, ...), condition=%wide.region_5.6_spmd.clone, body=%wide.region_1.5_spmd.clone.sunk | while | flops 277055616 | bytes 10018514 | solution.py:36
  170.3 1.0 constant_dynamic-slice_fusion.9
  172.1 1.0 select_reduce_fusion.2
  173.5 1.0 constant_dynamic-slice_fusion.9
  175.4 1.0 select_reduce_fusion.2
  176.8 1.0 constant_dynamic-slice_fusion.9
  178.6 1.0 select_reduce_fusion.2
  180.0 1.0 constant_dynamic-slice_fusion.9
  181.9 1.0 select_reduce_fusion.2
  182.9 38.2 %all-gather.7.cloned.1.call-done = bf16[2048,256]{1,0:T(8,128)(2,1)} async-done(((bf16[128,256]{1,0:T(8,128)(2,1)}), bf16[2048,256]{1,0:T(8,128)(2,1)}) %all-gather.7.cloned.1.call-update) | async-done | bytes 1048592 | tf_op jit(solution)/shard_map/all_gather | solution.py:93
  221.2 2.3 copy.102
  223.5 22.7 %while.58 = (s32[]{:T(128)}, f32[128,2,8,128]{0,3,2,1:T(8,128)}, bf16[2048,256]{0,1:T(8,128)(2,1)}, s32[1,4]{1,0:T(1,128)S(1)}, s32[128]{0:T(128)S(1)}, /*index=...) while((s32[]{:T(128)}, f32[128,2,8,128]{0,3,2,1:T(8,128)}, ...), condition=%wide.region_8.9_spmd.clone, body=%wide.region_6.8_spmd.clone.sunk | while | flops 541810816 | bytes 4349657 | solution.py:36
  223.8 1.8 constant_dynamic-slice_fusion.10
  225.6 3.3 fusion.98
  229.2 1.8 constant_dynamic-slice_fusion.10
  231.0 3.6 fusion.98
  235.0 1.8 constant_dynamic-slice_fusion.10
  236.7 3.6 fusion.98
  240.7 1.8 constant_dynamic-slice_fusion.10
  242.5 3.6 fusion.98
  246.1 2.4 multiply_reduce_fusion
  248.5 1.1 broadcast.1274.clone
  249.6 1.1 broadcast.1274
  250.8 32.6 %while.59 = (s32[]{:T(128)}, f32[128,2,8,128]{0,3,2,1:T(8,128)}, bf16[2048,256]{0,1:T(8,128)(2,1)}, bf16[2048,256]{0,1:T(8,128)(2,1)}, bf16[2048,256]{0,1:T(8,12...) while((s32[]{:T(128)}, f32[128,2,8,128]{0,3,2,1:T(8,128)}, ...), condition=%wide.region_12.13_spmd.clone, body=%wide.region_10.12_spmd.clone.sunk | while | flops 1353932928 | bytes 35102520 | solution.py:36
  251.1 1.0 constant_dynamic-slice_fusion.12
  254.8 1.5 fusion.110
  262.9 1.5 fusion.110
  268.4 1.0 constant_dynamic-slice_fusion.11
  271.1 1.5 fusion.110
  279.3 1.5 fusion.110
  283.4 2.3 copy.138
  285.7 2.3 copy.136
  288.3 83.3 %reduce-scatter.12.cloned.1.call-done = bf16[128,256]{1,0:T(8,128)(2,1)} async-done(((bf16[2048,256]{1,0:T(8,128)(2,1)}), bf16[128,256]{1,0:T(8,128)(2,1)}) %reduce-scatter.12.cloned.1.call-update) | async-done | bytes 65552
  372.5 87.5 %reduce-scatter.10.cloned.1.call-done = bf16[128,256]{1,0:T(8,128)(2,1)} async-done(((bf16[2048,256]{1,0:T(8,128)(2,1)}), bf16[128,256]{1,0:T(8,128)(2,1)}) %reduce-scatter.10.cloned.1.call-update) | async-done | bytes 65552
  461.0 8.1 convolution_bitcast_fusion.1
  469.1 1.0 copy-done.4
  470.1 1.0 copy.126
  471.1 1.3 convert_element_type.103
  472.4 1.0 copy.127
  473.4 413.3 %reduce-scatter.8.cloned.1.call-done = f32[128,512]{0,1:T(8,128)} async-done(((f32[8192,512]{0,1:T(8,128)}), f32[128,512]{0,1:T(8,128)}) %reduce-scatter.8.cloned.1.call-update) | async-done | bytes 262160 | tf_op jit(solution)/shard_map/reduce_scatter | solution.py:179
  886.8 1.0 fusion.50
  (155 shorter events, 36.6 us)
Async XLA Ops:
  7.2 52.6 %copy-start = (bf16[1,128,8192]{2,1,0:T(8,128)(2,1)S(1)}, bf16[1,128,8192]{2,1,0:T(8,128)(2,1)}, u32[]{:S(2)}) copy-start(bf16[1,128,8192]{2,1,0:T(8,128)(2,1)} %param.12) | copy-start | bytes 6291460
  7.2 56.2 %copy-start.5 = (bf16[1,128,2048]{2,1,0:T(8,128)(2,1)S(1)}, bf16[1,128,2048]{2,1,0:T(8,128)(2,1)}, u32[]{:S(2)}) copy-start(bf16[1,128,2048]{2,1,0:T(8,128)(2,1)} %param.13) | copy-start | bytes 1572868
  7.2 52.6 %all-gather.9.cloned.1.call-start = ((), (), s32[]{:S(2)}) async-start(), calls=%async_computation.5 | async-start | bytes 5242880 | tf_op jit(solution)/shard_map/all_gather | solution.py:59
  7.9 103.1 %all-gather.5.cloned.1.call-start = ((), (), s32[]{:S(2)}) async-start(), calls=%async_computation.3 | async-start | bytes 5242880 | tf_op jit(solution)/shard_map/all_gather | solution.py:60
  8.7 57.4 %copy-start.6 = (s32[1,4]{1,0:T(1,128)S(1)}, s32[1,4]{1,0:T(1,128)}, u32[]{:S(2)}) copy-start(s32[1,4]{1,0:T(1,128)} %param.17) | copy-start | bytes 52
  8.7 159.0 %all-gather.11.cloned.1.call-start = ((), (), s32[]{:S(2)}) async-start(), calls=%async_computation.6 | async-start | bytes 1114112 | tf_op jit(solution)/shard_map/all_gather | solution.py:92
  63.3 157.9 %all-gather.7.cloned.1.call-start = ((), (), s32[]{:S(2)}) async-start(), calls=%async_computation.4 | async-start | bytes 1114112 | tf_op jit(solution)/shard_map/all_gather | solution.py:93
  114.6 257.0 %reduce-scatter.12.cloned.1.call-start = ((), (), s32[]{:S(2)}) async-start(), calls=%async_computation.9 | async-start | bytes 1114112
  246.1 4.6 copy-start.3
  254.8 2.3 copy-start.1
  257.7 1.2 copy-start.2
  262.9 2.3 copy-start.1
  265.9 1.2 copy-start.2
  271.1 2.3 copy-start.1
  274.1 1.2 copy-start.2
  279.3 2.3 copy-start.1
  282.2 1.2 copy-start.2
  285.7 174.3 %reduce-scatter.10.cloned.1.call-start = ((), (), s32[]{:S(2)}) async-start(), calls=%async_computation.8 | async-start | bytes 1114112
  288.1 598.7 %reduce-scatter.8.cloned.1.call-start = ((), (), s32[]{:S(2)}) async-start(), calls=%async_computation.7 | async-start | bytes 17039360 | tf_op jit(solution)/shard_map/reduce_scatter | solution.py:179
  469.1 1.0 copy-start.4
Sparse Core Ops, SparseCore 0:
  9.8 49.9 all-gather.8
  61.6 49.4 all-gather.4
  114.0 53.6 all-gather.10
  170.6 50.5 all-gather.6
  285.8 85.6 reduce-scatter.11
  374.9 85.0 reduce-scatter.9
  469.2 417.5 reduce-scatter.7
where the time goes:
time: 897 us; the launch traced here: 896 us
  waiting for transfers between devices  773 us (86%)
  matrix products  51.1 us (6%)
  local copies, waits for them, and re-layouts  45 us (5%)
  between operations  14.3 us (2%)
  other arithmetic  11.9 us (1%)
    reduce_scatter x1, waiting for transfers between devices, on_device(): lax.psum_scatter(jnp.dot(columns.T, both_grads, preferred_element_type=jn...  413 us
    unnamed x9, waiting for transfers between devices  172 us
    all_gather x1, waiting for transfers between devices, on_device(): lax.all_gather(keys, 'cp', axis=0, tiled=True)  53.1 us
    all_gather x1, waiting for transfers between devices, on_device(): lax.all_gather(k_weight, 'dp', axis=0, tiled=True)  51 us
    all_gather x1, waiting for transfers between devices, on_device(): lax.all_gather(v_weight, 'dp', axis=0, tiled=True)  44.9 us
    all_gather x1, waiting for transfers between devices, on_device(): lax.all_gather(values, 'cp', axis=0, tiled=True)  38.2 us
  transfers between devices with their start and end apart: 7, of which 7 were waited for; matrix products, arithmetic and copies ran while one was open for 3% of the time, Pallas kernels for 0%

commit v1 on v0

--- a/solution.py
+++ b/solution.py
@@ -6,6 +6,14 @@
 
 DH = 128
 NEG_BIG = -1e30
+
+
+def store_surface_all(vector):
+    stack_in = []
+    for _ in range(lax.axis_size("dp")):
+        stack_in.append(vector)
+    main = jnp.concatenate(lax.all_to_all(jnp.stack(stack_in), "dp", 0, 0), axis=0)
+    return main
 
 
 def place(rows, tok_rows, seq_rows):
@@ -55,10 +63,7 @@
         key_doc = doc_index(key_place, starts)
         return (key_place[None, :] <= own_place[:, None]) & (key_doc[None, :] == own_doc[:, None])
 
-    pieces = (
-        lax.all_gather(k_weight, "dp", axis=0, tiled=True),
-        lax.all_gather(v_weight, "dp", axis=0, tiled=True),
-    )
+    pieces = (store_surface_all(k_weight), lax.all_gather(v_weight, "dp", axis=0, tiled=True))
     columns = inputs
     key_sums = jnp.dot(columns, pieces[0], preferred_element_type=jnp.float32)
     value_sums = jnp.dot(columns, pieces[1], preferred_element_type=jnp.float32)

time: 897 us -> 879 us (0.980)
  waiting for transfers between devices: 773 us -> 746 us
    all_to_all x0 -> x1, waiting for transfers between devices: none -> 72.1 us  [store_surface_all(): lax.all_to_all(jnp.stack(stack_in), 'dp', 0, 0)]
    all_gather x1 -> x0, waiting for transfers between devices: 51 us -> none  [on_device(): lax.all_gather(k_weight, 'dp', axis=0, tiled=True)]
    all_gather x1, waiting for transfers between devices: 44.9 us -> 0.82 us  [on_device(): lax.all_gather(v_weight, 'dp', axis=0, tiled=True)]
    unnamed x9 -> x8, waiting for transfers between devices: 172 us -> 172 us
  transfers between devices with their start and end apart: 7 -> 7, of which waited for: 7 -> 7; matrix products, arithmetic and copies ran while one was open for 3% -> 4% of each run, Pallas kernels for 0% -> 0%
where the time goes in v1:
time: 879 us; the launch traced here: 878 us
  waiting for transfers between devices  746 us (85%)
  matrix products  51.1 us (6%)
  local copies, waits for them, and re-layouts  48.5 us (6%)
  between operations  14.2 us (2%)
  other arithmetic  11.9 us (1%)
    reduce_scatter x1, waiting for transfers between devices, on_device(): lax.psum_scatter(jnp.dot(columns.T, both_grads, preferred_element_type=jn...  408 us
    unnamed x8, waiting for transfers between devices  172 us
    all_to_all x1, waiting for transfers between devices, store_surface_all(): lax.all_to_all(jnp.stack(stack_in), 'dp', 0, 0)  72.1 us
    all_gather x1, waiting for transfers between devices, on_device(): lax.all_gather(keys, 'cp', axis=0, tiled=True)  55.1 us
    all_gather x1, waiting for transfers between devices, on_device(): lax.all_gather(values, 'cp', axis=0, tiled=True)  38.4 us
  transfers between devices with their start and end apart: 7, of which 7 were waited for; matrix products, arithmetic and copies ran while one was open for 4% of the time, Pallas kernels for 0%

profile of v1, /device:TPU:36, one launch (start us, length us, event | category | flops | bytes accessed | tf_op | source)
XLA Modules:
  0.0 878.0 jit_solution(5522082415263649437)
XLA Ops:
  7.2 3.6 stack.2
  10.8 4.9 all-to-all-start
  16.5 72.1 %all-to-all-done = bf16[4,2048,256]{2,1,0:T(8,128)(2,1)} async-done(((bf16[4,2048,256]{2,1,0:T(8,128)(2,1)}), bf16[4,2048,256]{2,1,0:T(8,128)(2,1)}, u32[]{:S(2)}, u32[]{:S(2)}) %all-to-all-start) | async-done | bytes 4194336 | tf_op jit(solution)/shard_map/all_to_all | solution.py:15
  88.6 3.5 fusion.43
  92.8 2.0 copy.106
  95.8 3.5 fusion.40
  99.4 55.1 %all-gather.8.cloned.1.call-done = bf16[2048,256]{1,0:T(8,128)(2,1)} async-done(((bf16[128,256]{1,0:T(8,128)(2,1)}), bf16[2048,256]{1,0:T(8,128)(2,1)}) %all-gather.8.cloned.1.call-update) | async-done | bytes 1048592 | tf_op jit(solution)/shard_map/all_gather | solution.py:97
  154.5 2.3 copy.103
  156.7 13.0 %while.57 = (s32[]{:T(128)}, f32[2,8,128]{2,1,0:T(8,128)S(1)}, f32[2,8,128]{2,1,0:T(8,128)S(1)}, s32[1,4]{1,0:T(1,128)S(1)}, s32[128]{0:T(128)S(1)}, /*index=5*/...) while((s32[]{:T(128)}, f32[2,8,128]{2,1,0:T(8,128)S(1)}, ...), condition=%wide.region_5.6_spmd.clone, body=%wide.region_1.5_spmd.clone.sunk | while | flops 277055616 | bytes 10018514 | solution.py:44
  157.1 1.0 constant_dynamic-slice_fusion.9
  158.9 1.0 select_reduce_fusion.2
  160.3 1.0 constant_dynamic-slice_fusion.9
  162.2 1.0 select_reduce_fusion.2
  163.6 1.0 constant_dynamic-slice_fusion.9
  165.4 1.0 select_reduce_fusion.2
  168.7 1.0 select_reduce_fusion.2
  169.7 38.4 %all-gather.6.cloned.1.call-done = bf16[2048,256]{1,0:T(8,128)(2,1)} async-done(((bf16[128,256]{1,0:T(8,128)(2,1)}), bf16[2048,256]{1,0:T(8,128)(2,1)}) %all-gather.6.cloned.1.call-update) | async-done | bytes 1048592 | tf_op jit(solution)/shard_map/all_gather | solution.py:98
  208.1 2.3 copy.102
  210.4 22.7 %while.58 = (s32[]{:T(128)}, f32[128,2,8,128]{0,3,2,1:T(8,128)}, bf16[2048,256]{0,1:T(8,128)(2,1)}, s32[1,4]{1,0:T(1,128)S(1)}, s32[128]{0:T(128)S(1)}, /*index=...) while((s32[]{:T(128)}, f32[128,2,8,128]{0,3,2,1:T(8,128)}, ...), condition=%wide.region_8.9_spmd.clone, body=%wide.region_6.8_spmd.clone.sunk | while | flops 541810816 | bytes 4349657 | solution.py:44
  210.7 1.8 constant_dynamic-slice_fusion.10
  212.5 3.3 fusion.98
  216.1 1.8 constant_dynamic-slice_fusion.10
  217.9 3.7 fusion.98
  221.9 1.8 constant_dynamic-slice_fusion.10
  223.7 3.7 fusion.98
  227.7 1.8 constant_dynamic-slice_fusion.10
  229.5 3.7 fusion.98
  233.1 2.4 multiply_reduce_fusion
  235.5 1.1 broadcast.1276.clone
  236.6 1.1 broadcast.1276
  237.7 32.6 %while.59 = (s32[]{:T(128)}, f32[128,2,8,128]{0,3,2,1:T(8,128)}, bf16[2048,256]{0,1:T(8,128)(2,1)}, bf16[2048,256]{0,1:T(8,128)(2,1)}, bf16[2048,256]{0,1:T(8,12...) while((s32[]{:T(128)}, f32[128,2,8,128]{0,3,2,1:T(8,128)}, ...), condition=%wide.region_12.13_spmd.clone, body=%wide.region_10.12_spmd.clone.sunk | while | flops 1353932928 | bytes 35102520 | solution.py:44
  238.0 1.0 constant_dynamic-slice_fusion.12
  239.0 1.0 constant_dynamic-slice_fusion.11
  241.7 1.5 fusion.110
  249.9 1.5 fusion.110
  258.1 1.5 fusion.110
  266.2 1.5 fusion.110
  270.3 2.3 copy.138
  272.7 2.3 copy.136
  275.2 83.2 %reduce-scatter.12.cloned.1.call-done = bf16[128,256]{1,0:T(8,128)(2,1)} async-done(((bf16[2048,256]{1,0:T(8,128)(2,1)}), bf16[128,256]{1,0:T(8,128)(2,1)}) %reduce-scatter.12.cloned.1.call-update) | async-done | bytes 65552
  359.4 87.5 %reduce-scatter.10.cloned.1.call-done = bf16[128,256]{1,0:T(8,128)(2,1)} async-done(((bf16[2048,256]{1,0:T(8,128)(2,1)}), bf16[128,256]{1,0:T(8,128)(2,1)}) %reduce-scatter.10.cloned.1.call-update) | async-done | bytes 65552
  447.8 8.1 convolution_bitcast_fusion.1
  455.9 1.0 copy-done.4
  456.9 1.0 copy.126
  457.9 1.3 convert_element_type.103
  459.3 1.0 copy.127
  460.3 408.3 %reduce-scatter.8.cloned.1.call-done = f32[128,512]{0,1:T(8,128)} async-done(((f32[8192,512]{0,1:T(8,128)}), f32[128,512]{0,1:T(8,128)}) %reduce-scatter.8.cloned.1.call-update) | async-done | bytes 262160 | tf_op jit(solution)/shard_map/reduce_scatter | solution.py:184
  868.6 1.0 fusion.50
  (155 shorter events, 37.7 us)
Async XLA Ops:
  7.2 81.4 %copy-start = (bf16[1,128,8192]{2,1,0:T(8,128)(2,1)S(1)}, bf16[1,128,8192]{2,1,0:T(8,128)(2,1)}, u32[]{:S(2)}) copy-start(bf16[1,128,8192]{2,1,0:T(8,128)(2,1)} %param.12) | copy-start | bytes 6291460
  10.8 77.8 %all-to-all-start = ((bf16[4,2048,256]{2,1,0:T(8,128)(2,1)}), bf16[4,2048,256]{2,1,0:T(8,128)(2,1)}, u32[]{:S(2)}, u32[]{:S(2)}) async-start(bf16[4,2048,256]{2,1,0:T(8,128)(2,1)} %stack.2), calls=%async_computation | async-start | bytes 8388608 | tf_op jit(solution)/shard_map/all_to_all | solution.py:15
  15.7 76.6 %copy-start.5 = (bf16[1,128,2048]{2,1,0:T(8,128)(2,1)S(1)}, bf16[1,128,2048]{2,1,0:T(8,128)(2,1)}, u32[]{:S(2)}) copy-start(bf16[1,128,2048]{2,1,0:T(8,128)(2,1)} %param.13) | copy-start | bytes 1572868
  15.7 80.1 %all-gather.4.cloned.1.call-start = ((), (), s32[]{:S(2)}) async-start(), calls=%async_computation.4 | async-start | bytes 5242880 | tf_op jit(solution)/shard_map/all_gather | solution.py:66
  16.4 138.1 %all-gather.8.cloned.1.call-start = ((), (), s32[]{:S(2)}) async-start(), calls=%async_computation.6 | async-start | bytes 1114112 | tf_op jit(solution)/shard_map/all_gather | solution.py:97
  88.6 6.3 copy-start.6
  92.1 116.0 %all-gather.6.cloned.1.call-start = ((), (), s32[]{:S(2)}) async-start(), calls=%async_computation.5 | async-start | bytes 1114112 | tf_op jit(solution)/shard_map/all_gather | solution.py:98
  99.4 259.1 %reduce-scatter.12.cloned.1.call-start = ((), (), s32[]{:S(2)}) async-start(), calls=%async_computation.9 | async-start | bytes 1114112
  233.1 4.6 copy-start.3
  241.7 2.3 copy-start.1
  244.7 1.2 copy-start.2
  249.9 2.3 copy-start.1
  252.8 1.2 copy-start.2
  258.0 2.3 copy-start.1
  261.0 1.2 copy-start.2
  266.2 2.3 copy-start.1
  269.1 1.2 copy-start.2
  272.6 174.2 %reduce-scatter.10.cloned.1.call-start = ((), (), s32[]{:S(2)}) async-start(), calls=%async_computation.8 | async-start | bytes 1114112
  275.0 593.6 %reduce-scatter.8.cloned.1.call-start = ((), (), s32[]{:S(2)}) async-start(), calls=%async_computation.7 | async-start | bytes 17039360 | tf_op jit(solution)/shard_map/reduce_scatter | solution.py:184
  455.9 1.0 copy-start.4
Sparse Core Ops, SparseCore 0:
  18.3 77.4 all-gather.3
  98.8 55.6 all-gather.7
  157.5 50.5 all-gather.5
  272.8 85.6 reduce-scatter.11
  361.8 85.0 reduce-scatter.9
  456.0 412.5 reduce-scatter.7
